TPU v7x, 512 devices: a whole 4x8x8 slice. The times are simulated.
512 devices in a mesh: worker: 16 (over x, z_lo, core), fsdp: 32 (over z_hi, y).
Axes of the slice: x: 4, y: 8, z: 8 (z_hi: 4, z_lo: 2; z = z_hi * 2 + z_lo), core: 2. Of those that a mesh axis runs over, the one named last changes fastest.
Arguments:
- hidden: bfloat16 [9472, 65536], P('fsdp', 'worker'), may hold values from -6 to 6
- cotangent: bfloat16 [65536, 1792], P(('worker', 'fsdp')), may hold values from -6 to 6
- first_moment: bfloat16 [16, 9472, 1792], P('worker', 'fsdp'), may hold values from -0.0625 to 0.0625
- second_moment: bfloat16 [16, 9472, 1792], P('worker', 'fsdp'), may hold values from 1.21593475e-05 to 0.00024414062
- outer_momentum: bfloat16 [9472, 1792], P('fsdp', 'worker'), may hold values from -4 to 4
Outputs:
- new_momentum: float32 [9472, 1792], P('fsdp', 'worker')
All inputs are finite; a program needn't handle non-finite values.
Results may differ from a plain program's by a relative error of at most 0.0003.
Values may be sent and summed in bfloat16 or wider, within the bound.
No kernel may reach another device: no remote copies, remote signals or barrier semaphores. Data moves between devices by JAX's collectives and lax.ppermute only.
A program may use at most 64 MiB of HBM per device.

v0:
```python
import jax
import jax.numpy as jnp
from jax import lax
from jax.sharding import Mesh
from jax.sharding import PartitionSpec as P

W = ("wx", "wz", "wc")
F = ("fz", "fy")


def shards(hidden, cotangent, first_moment, second_moment, outer_momentum):
    gathered = lax.all_gather(cotangent, "fy", axis=0, tiled=True)
    gathered = lax.all_gather(gathered, "fz", axis=0, tiled=True)
    gradient = jnp.dot(hidden, gathered, preferred_element_type=jnp.float32) / gathered.shape[0]
    first_new = 0.9 * first_moment[0].astype(jnp.float32) + 0.1 * gradient
    second_new = 0.95 * second_moment[0].astype(jnp.float32) + 0.05 * gradient * gradient
    pseudo = first_new / (jnp.sqrt(second_new) + 1e-08)
    summed = lax.psum_scatter(pseudo, "wx", scatter_dimension=1, tiled=True)
    summed = lax.psum_scatter(summed, "wz", scatter_dimension=1, tiled=True)
    summed = lax.psum_scatter(summed, "wc", scatter_dimension=1, tiled=True)
    average = summed / 16
    return 0.9 * outer_momentum.astype(jnp.float32) + average


def solution(mesh):
    sizes = {"worker": (4, 2, 2), "fsdp": (4, 8)}
    fine = Mesh(mesh.devices.reshape(sizes["worker"] + sizes["fsdp"]), W + F)
    in_specs = (P(F, W), P(W + F, None), P(W, F, None), P(W, F, None), P(F, W))
    out_specs = P(F, W)
    return jax.shard_map(shards, mesh=fine, in_specs=in_specs, out_specs=out_specs, check_vma=False)
```

profile of v0, /device:TPU:1, one launch (start us, length us, event | category | flops | bytes accessed | tf_op | source)
XLA Modules:
  0.0 440.6 jit_solution(18052096988505240915)
XLA Ops:
  6.5 0.0 copy-start
  6.5 0.0 all-gather.3.cloned.1.call-start
  6.5 0.7 all-gather.3.cloned.1.call-update
  7.3 0.0 all-gather.5.cloned.1.call-start
  7.3 59.6 %all-gather.3.cloned.1.call-done = bf16[1024,1792]{1,0:T(8,128)(2,1)} async-done(((bf16[128,1792]{1,0:T(8,128)(2,1)}), bf16[1024,1792]{1,0:T(8,128)(2,1)}) %all-gather.3.cloned.1.call-update) | async-done | bytes 3670032 | tf_op jit(solution)/shard_map/all_gather | solution.py:12
  66.9 0.0 all-gather.5.cloned.1.call-update
  66.9 0.0 reduce-scatter.10.cloned.1.call-start
  67.0 263.2 %all-gather.5.cloned.1.call-done = bf16[4096,1792]{1,0:T(8,128)(2,1)} async-done(((bf16[1024,1792]{1,0:T(8,128)(2,1)}), bf16[4096,1792]{1,0:T(8,128)(2,1)}) %all-gather.5.cloned.1.call-update) | async-done | bytes 14680080 | tf_op jit(solution)/shard_map/all_gather | solution.py:13
  330.2 0.0 copy-done
  330.2 12.5 %fusion.2 = f32[296,1792]{1,0:T(8,128)} fusion(bf16[1,296,1792]{2,1,0:T(8,128)(2,1)} %param.8, bf16[1,296,1792]{2,1,0:T(8,128)(2,1)} %param.7, bf16[296,4096]{1,0:T(8,128)(2,1)S(1)} %copy-done, bf16[4096,1792]{1,0:T(8,128)(2,1)} %all-gather.5.cloned.1.call-done), kind=kOutput, calls=%fused_computation.3 | convolution fusion | flops 4351664128 | bytes 21348352 | tf_op jit(solution)/shard_map/dot_general | solution.py:14
  342.7 3.2 copy.6
  345.9 0.0 copy-start.1
  345.9 0.0 reduce-scatter.10.cloned.1.call-update
  345.9 0.0 reduce-scatter.12.cloned.1.call-start
  346.0 38.9 %reduce-scatter.10.cloned.1.call-done = f32[448,296]{1,0:T(8,128)} async-done(((f32[1792,296]{1,0:T(8,128)}), f32[448,296]{1,0:T(8,128)}) %reduce-scatter.10.cloned.1.call-update) | async-done | bytes 530448
  384.9 0.0 reduce-scatter.12.cloned.1.call-update
  384.9 0.0 reduce-scatter.14.cloned.1.call-start
  384.9 26.8 %reduce-scatter.12.cloned.1.call-done = f32[224,296]{1,0:T(8,128)} async-done(((f32[448,296]{1,0:T(8,128)}), f32[224,296]{1,0:T(8,128)}) %reduce-scatter.12.cloned.1.call-update) | async-done | bytes 265232
  411.7 0.0 reduce-scatter.14.cloned.1.call-update
  411.7 20.6 %reduce-scatter.14.cloned.1.call-done = f32[112,296]{1,0:T(8,128)} async-done(((f32[224,296]{1,0:T(8,128)}), f32[112,296]{1,0:T(8,128)}) %reduce-scatter.14.cloned.1.call-update) | async-done | bytes 132624
  432.3 1.0 copy.11
  433.3 0.0 copy-done.1
  433.4 0.7 multiply_add_fusion
Async XLA Ops:
  6.5 323.6 %copy-start = (bf16[296,4096]{1,0:T(8,128)(2,1)S(1)}, bf16[296,4096]{1,0:T(8,128)(2,1)}, u32[]{:S(2)}) copy-start(bf16[296,4096]{1,0:T(8,128)(2,1)} %param.5) | copy-start | bytes 7274500
  6.5 60.4 %all-gather.3.cloned.1.call-start = ((), (), s32[]{:S(2)}) async-start(), calls=%async_computation.3 | async-start | bytes 4128768 | tf_op jit(solution)/shard_map/all_gather | solution.py:12
  7.3 322.9 %all-gather.5.cloned.1.call-start = ((), (), s32[]{:S(2)}) async-start(), calls=%async_computation.4 | async-start | bytes 18350080 | tf_op jit(solution)/shard_map/all_gather | solution.py:13
  66.9 317.9 %reduce-scatter.10.cloned.1.call-start = ((), (), s32[]{:S(2)}) async-start(), calls=%async_computation.5 | async-start | bytes 3440640
  345.9 87.5 %copy-start.1 = (bf16[296,112]{1,0:T(8,128)(2,1)S(1)}, bf16[296,112]{1,0:T(8,128)(2,1)}, u32[]{:S(2)}) copy-start(bf16[296,112]{1,0:T(8,128)(2,1)} %param.9) | copy-start | bytes 198916
  345.9 65.8 %reduce-scatter.12.cloned.1.call-start = ((), (), s32[]{:S(2)}) async-start(), calls=%async_computation.6 | async-start | bytes 1032192
  384.9 47.4 %reduce-scatter.14.cloned.1.call-start = ((), (), s32[]{:S(2)}) async-start(), calls=%async_computation.7 | async-start | bytes 516096
Sparse Core Ops, SparseCore 0:
  9.4 57.4 all-gather.2
  69.0 261.1 all-gather.4
  346.0 38.7 reduce-scatter.9
  387.5 24.1 reduce-scatter.11
  414.3 17.9 reduce-scatter.13
where the time goes:
time: 441 us
  waiting for transfers between devices  410 us (93%)
  between operations  13.2 us (3%)
  matrix products  12.5 us (3%)
    all_gather x1, waiting for transfers between devices, shards(): gathered = lax.all_gather(gathered, 'fz', axis=0, tiled=True)  263 us
    unnamed x8, waiting for transfers between devices  87.1 us
    all_gather x1, waiting for transfers between devices, shards(): gathered = lax.all_gather(cotangent, 'fy', axis=0, tiled=True)  59.6 us
    dot_general x1, matrix products, shards(): jnp.dot(hidden, gathered, preferred_element_type=jnp.float32)  12.5 us
  transfers between devices with their start and end apart: 5, of which 5 were waited for; matrix products, arithmetic and copies ran while one was open for 0% of the time, Pallas kernels for 0%

commit v1 on v0

--- a/solution.py
+++ b/solution.py
@@ -9,7 +9,9 @@
 
 
 def shards(hidden, cotangent, first_moment, second_moment, outer_momentum):
-    gathered = lax.all_gather(cotangent, "fy", axis=0, tiled=True)
+    gathered = jnp.concatenate(
+        lax.all_to_all(jnp.stack([cotangent] * lax.axis_size("fy")), "fy", 0, 0), axis=0
+    )
     gathered = lax.all_gather(gathered, "fz", axis=0, tiled=True)
     gradient = jnp.dot(hidden, gathered, preferred_element_type=jnp.float32) / gathered.shape[0]
     first_new = 0.9 * first_moment[0].astype(jnp.float32) + 0.1 * gradient

time: 441 us -> 474 us (1.075)
  blocking collectives: 0 us -> 89.5 us
  waiting for transfers between devices: 410 us -> 352 us
    all_to_all x0 -> x1, blocking collectives: none -> 89.5 us  [shards(): lax.all_to_all(jnp.stack([cotangent] * lax.axis_size('fy')), 'fy', 0, 0)]
    all_gather x1 -> x0, waiting for transfers between devices: 59.6 us -> none  [shards(): gathered = lax.all_gather(cotangent, 'fy', axis=0, tiled=True)]
    unnamed x8 -> x7, waiting for transfers between devices: 87.1 us -> 87.1 us
  transfers between devices with their start and end apart: 5 -> 4, of which waited for: 5 -> 4; matrix products, arithmetic and copies ran while one was open for 0% -> 0% of each run, Pallas kernels for 0% -> 0%
where the time goes in v1:
time: 474 us; the launch traced here: 473 us
  waiting for transfers between devices  352 us (74%)
  blocking collectives  89.5 us (19%)
  between operations  13.2 us (3%)
  matrix products  12.5 us (3%)
  local copies, waits for them, and re-layouts  5.65 us (1%)
    all_gather x1, waiting for transfers between devices, shards(): gathered = lax.all_gather(gathered, 'fz', axis=0, tiled=True)  265 us
    all_to_all x1, blocking collectives, shards(): lax.all_to_all(jnp.stack([cotangent] * lax.axis_size('fy')), 'fy', 0, 0)  89.5 us
    unnamed x7, waiting for transfers between devices  87.1 us
    dot_general x1, matrix products, shards(): jnp.dot(hidden, gathered, preferred_element_type=jnp.float32)  12.5 us
  transfers between devices with their start and end apart: 4, of which 4 were waited for; matrix products, arithmetic and copies ran while one was open for 0% of the time, Pallas kernels for 0%

profile of v1, /device:TPU:1, one launch (start us, length us, event | category | flops | bytes accessed | tf_op | source)
XLA Modules:
  0.0 473.4 jit_solution(2690406624657570414)
XLA Ops:
  6.5 0.0 copy-start
  6.5 0.0 all-gather.2.cloned.1.call-start
  6.5 1.4 stack.2
  8.0 89.5 %all_to_all.5 = bf16[8,128,1792]{2,1,0:T(8,128)(2,1)} all-to-all(bf16[8,128,1792]{2,1,0:T(8,128)(2,1)S(1)} %stack.2), channel_id=1, replica_groups=mesh['wx'=4,'wz'=2,'wc'=2,'fz'=4,'fy'=8] {'fy'}, dimensions={0} | all-to-all | bytes 7340032 | tf_op jit(solution)/shard_map/all_to_all | solution.py:13
  97.4 0.0 all-gather.2.cloned.1.call-update
  97.4 0.0 reduce-scatter.10.cloned.1.call-start
  97.5 264.7 %all-gather.2.cloned.1.call-done = bf16[4096,1792]{1,0:T(8,128)(2,1)} async-done(((bf16[1024,1792]{1,0:T(8,128)(2,1)}), bf16[4096,1792]{1,0:T(8,128)(2,1)}) %all-gather.2.cloned.1.call-update) | async-done | bytes 14680080 | tf_op jit(solution)/shard_map/all_gather | solution.py:15
  362.2 0.0 copy-done
  362.2 12.5 %fusion.2 = f32[296,1792]{1,0:T(8,128)} fusion(bf16[1,296,1792]{2,1,0:T(8,128)(2,1)} %param.8, bf16[1,296,1792]{2,1,0:T(8,128)(2,1)} %param.7, bf16[296,4096]{1,0:T(8,128)(2,1)S(1)} %copy-done, bf16[4096,1792]{1,0:T(8,128)(2,1)} %all-gather.2.cloned.1.call-done), kind=kOutput, calls=%fused_computation.3 | convolution fusion | flops 4351664128 | bytes 21348352 | tf_op jit(solution)/shard_map/dot_general | solution.py:16
  374.7 3.2 copy.6
  377.9 0.0 copy-start.1
  377.9 0.0 reduce-scatter.10.cloned.1.call-update
  377.9 0.0 reduce-scatter.12.cloned.1.call-start
  378.0 39.5 %reduce-scatter.10.cloned.1.call-done = f32[448,296]{1,0:T(8,128)} async-done(((f32[1792,296]{1,0:T(8,128)}), f32[448,296]{1,0:T(8,128)}) %reduce-scatter.10.cloned.1.call-update) | async-done | bytes 530448
  417.5 0.0 reduce-scatter.12.cloned.1.call-update
  417.5 0.0 reduce-scatter.14.cloned.1.call-start
  417.6 26.9 %reduce-scatter.12.cloned.1.call-done = f32[224,296]{1,0:T(8,128)} async-done(((f32[448,296]{1,0:T(8,128)}), f32[224,296]{1,0:T(8,128)}) %reduce-scatter.12.cloned.1.call-update) | async-done | bytes 265232
  444.5 0.0 reduce-scatter.14.cloned.1.call-update
  444.5 20.6 %reduce-scatter.14.cloned.1.call-done = f32[112,296]{1,0:T(8,128)} async-done(((f32[224,296]{1,0:T(8,128)}), f32[112,296]{1,0:T(8,128)}) %reduce-scatter.14.cloned.1.call-update) | async-done | bytes 132624
  465.1 1.0 copy.11
  466.1 0.0 copy-done.1
  466.1 0.7 multiply_add_fusion
Async XLA Ops:
  6.5 355.7 %copy-start = (bf16[296,4096]{1,0:T(8,128)(2,1)S(1)}, bf16[296,4096]{1,0:T(8,128)(2,1)}, u32[]{:S(2)}) copy-start(bf16[296,4096]{1,0:T(8,128)(2,1)} %param.5) | copy-start | bytes 7274500
  6.5 355.7 %all-gather.2.cloned.1.call-start = ((), (), s32[]{:S(2)}) async-start(), calls=%async_computation.4 | async-start | bytes 18350080 | tf_op jit(solution)/shard_map/all_gather | solution.py:15
  97.4 320.1 %reduce-scatter.10.cloned.1.call-start = ((), (), s32[]{:S(2)}) async-start(), calls=%async_computation.5 | async-start | bytes 3440640
  377.9 88.2 %copy-start.1 = (bf16[296,112]{1,0:T(8,128)(2,1)S(1)}, bf16[296,112]{1,0:T(8,128)(2,1)}, u32[]{:S(2)}) copy-start(bf16[296,112]{1,0:T(8,128)(2,1)} %param.9) | copy-start | bytes 198916
  377.9 66.5 %reduce-scatter.12.cloned.1.call-start = ((), (), s32[]{:S(2)}) async-start(), calls=%async_computation.6 | async-start | bytes 1032192
  417.5 47.6 %reduce-scatter.14.cloned.1.call-start = ((), (), s32[]{:S(2)}) async-start(), calls=%async_computation.7 | async-start | bytes 516096
Sparse Core Ops, SparseCore 0:
  97.6 264.5 all-gather.1
  378.1 39.3 reduce-scatter.9
  420.3 24.1 reduce-scatter.11
  447.1 17.9 reduce-scatter.13
